TPU v7x, 512 devices: a whole 4x4x16 slice. The times are simulated.
512 devices in a mesh: row: 32 (over z, core), col: 16 (over y, x).
Axes of the slice: x: 4, y: 4, z: 16, core: 2. Of those that a mesh axis runs over, the one named last changes fastest.
Arguments:
- tokens: bfloat16 [512, 8192], P('row', 'col'), may hold values from -6 to 6
- out_grad: bfloat16 [512, 8192], P('row', 'col'), may hold values from -1.5 to 1.5
- gate_weight: bfloat16 [8192, 16384], P('col', 'row'), may hold values from -0.0625 to 0.0625
- up_weight: bfloat16 [8192, 16384], P('col', 'row'), may hold values from -0.0625 to 0.0625
- down_weight: bfloat16 [16384, 8192], P('row', 'col'), may hold values from -0.046875 to 0.046875
Outputs:
- input_grad: bfloat16 [512, 8192], P('row', 'col')
- gate_weight_grad: bfloat16 [8192, 16384], P('col', 'row')
- up_weight_grad: bfloat16 [8192, 16384], P('col', 'row')
- down_weight_grad: bfloat16 [16384, 8192], P('row', 'col')
All inputs are finite; a program needn't handle non-finite values.
Results may differ from a plain program's by a relative error of at most 0.005.
Values may be sent and summed in bfloat16 or wider, within the bound.
No kernel may reach another device: no remote copies, remote signals or barrier semaphores. Data moves between devices by JAX's collectives and lax.ppermute only.
A program may use at most 64 MiB of HBM per device.

v0:
```python
import jax
import jax.numpy as jnp
from jax import lax
from jax.sharding import PartitionSpec as P


def pointwise(gate, up, hidden_grad):
    sig = jax.nn.sigmoid(gate)
    act = gate * sig
    hidden = (act * up).astype(jnp.bfloat16)
    gate_grad = (hidden_grad * up * sig * (1.0 + gate * (1.0 - sig))).astype(jnp.bfloat16)
    up_grad = (hidden_grad * act).astype(jnp.bfloat16)
    return (hidden, gate_grad, up_grad)


def body(tokens, out_grad, gate_weight, up_weight, down_weight):
    n_col = lax.psum(1, "col")
    n_row = lax.psum(1, "row")
    rows_all = lax.all_gather(tokens, "row", axis=0, tiled=True)
    grads_all = lax.all_gather(out_grad, "row", axis=0, tiled=True)
    n_tok, width = rows_all.shape
    contract_cols = (((1,), (1,)), ((), ()))
    contract_rows = (((0,), (0,)), ((), ()))
    gate_part = jnp.dot(rows_all, gate_weight, preferred_element_type=jnp.float32)
    up_part = jnp.dot(rows_all, up_weight, preferred_element_type=jnp.float32)
    grad_part = lax.dot_general(
        grads_all, down_weight, contract_cols, preferred_element_type=jnp.float32
    )
    hid = gate_part.shape[1]
    chunk = n_tok // n_col
    parts = jnp.stack([gate_part, up_part, grad_part]).reshape(3, n_col, chunk, hid)
    parts = lax.all_to_all(parts, "col", 1, 1, tiled=True)
    gate, up, hidden_grad = parts.sum(axis=1)
    small = jnp.stack(pointwise(gate, up, hidden_grad))
    spread = jnp.broadcast_to(small[None], (n_col,) + small.shape)
    spread = lax.all_to_all(spread, "col", 0, 0, tiled=True)
    spread = spread.transpose(1, 0, 2, 3).reshape(3, n_tok, hid)
    hidden, gate_grad, up_grad = (spread[0], spread[1], spread[2])
    gate_weight_grad = lax.dot_general(
        rows_all, gate_grad, contract_rows, preferred_element_type=jnp.float32
    ).astype(jnp.bfloat16)
    up_weight_grad = lax.dot_general(
        rows_all, up_grad, contract_rows, preferred_element_type=jnp.float32
    ).astype(jnp.bfloat16)
    down_weight_grad = lax.dot_general(
        hidden, grads_all, contract_rows, preferred_element_type=jnp.float32
    ).astype(jnp.bfloat16)
    total = lax.dot_general(
        gate_grad, gate_weight, contract_cols, preferred_element_type=jnp.float32
    ) + lax.dot_general(up_grad, up_weight, contract_cols, preferred_element_type=jnp.float32)
    total = total.reshape(n_row, n_tok // n_row, width)
    input_grad = lax.all_to_all(total, "row", 0, 0, tiled=True).sum(axis=0)
    return (input_grad.astype(jnp.bfloat16), gate_weight_grad, up_weight_grad, down_weight_grad)


def solution(mesh):
    return jax.shard_map(
        body,
        mesh=mesh,
        in_specs=(
            P("row", "col"),
            P("row", "col"),
            P("col", "row"),
            P("col", "row"),
            P("row", "col"),
        ),
        out_specs=(P("row", "col"), P("col", "row"), P("col", "row"), P("row", "col")),
        check_vma=False,
    )
```

profile of v0, /device:TPU:1, one launch (start us, length us, event | category | flops | bytes accessed | tf_op | source)
XLA Modules:
  0.0 213.3 jit_solution(18360959105764189668)
XLA Ops:
  0.6 0.0 copy-start
  0.6 0.0 copy-start.3
  0.7 39.4 %all_gather.6 = bf16[512,512]{1,0:T(8,128)(2,1)S(1)} all-gather(bf16[16,512]{1,0:T(8,128)(2,1)} %param.5), channel_id=1, replica_groups=mesh['row'=32,'col'=16] {'row'}, dimensions={0}, use_global_device_ids=true | all-gather | bytes 540672 | tf_op jit(solution)/shard_map/all_gather | solution.py:19
  40.0 28.7 %all_gather.7 = bf16[512,512]{1,0:T(8,128)(2,1)S(1)} all-gather(bf16[16,512]{1,0:T(8,128)(2,1)} %param.6), channel_id=1, replica_groups=mesh['row'=32,'col'=16] {'row'}, dimensions={0}, use_global_device_ids=true | all-gather | bytes 540672 | tf_op jit(solution)/shard_map/all_gather | solution.py:20
  68.8 1.5 fusion.5
  70.3 0.0 copy-done
  70.3 0.4 fusion.4
  70.7 0.0 copy-done.3
  70.7 0.5 fusion.6
  71.2 0.5 pad_maximum_fusion
  71.7 45.6 %all_to_all.15 = f32[3,16,32,512]{3,2,0,1:T(8,128)} all-to-all(f32[3,16,32,512]{3,2,0,1:T(8,128)S(1)} %pad_maximum_fusion), channel_id=1, replica_groups=mesh['row'=32,'col'=16] {'col'}, dimensions={1} | all-to-all | bytes 6291456 | tf_op jit(solution)/shard_map/all_to_all | solution.py:32
  117.4 2.2 %reduce_sum.18 = f32[3,32,512]{2,1,0:T(8,128)S(1)} reduce(f32[3,16,32,512]{3,2,0,1:T(8,128)} %all_to_all.15, f32[]{:T(128)} %constant.0.clone.1), dimensions={1}, to_apply=%region_0.0 | reduce | flops 737280 | bytes 3342340 | tf_op jit(solution)/shard_map/reduce_sum | solution.py:33
  119.6 0.2 broadcast_in_dim.2
  119.8 24.6 %all_to_all.16 = bf16[16,3,32,512]{3,2,1,0:T(8,128)(2,1)S(1)} all-to-all(bf16[16,3,32,512]{3,2,1,0:T(8,128)(2,1)S(1)} %broadcast_in_dim.2), channel_id=1, replica_groups=mesh['row'=32,'col'=16] {'col'}, dimensions={0} | all-to-all | bytes 3145728 | tf_op jit(solution)/shard_map/all_to_all | solution.py:36
  144.4 0.0 copy-start.1
  144.4 0.9 fusion.3
  145.3 0.0 copy-start.2
  145.3 0.5 fusion.7
  145.8 0.0 copy-done.1
  145.8 1.4 convolution_add_fusion
  147.3 0.0 copy-done.2
  147.3 9.6 %all-to-all-start.2 = ((f32[32,16,512]{2,1,0:T(8,128)}), f32[32,16,512]{2,1,0:T(8,128)S(1)}, u32[]{:S(2)}, u32[]{:S(2)}) async-start(f32[32,16,512]{2,1,0:T(8,128)} %bitcast.9), calls=%async_computation.2 | async-start | bytes 2097152 | tf_op jit(solution)/shard_map/all_to_all | solution.py:52
  156.9 2.3 %fusion = bf16[512,512]{0,1:T(8,128)(2,1)} fusion(bf16[512,512]{1,0:T(8,128)(2,1)} %bitcast.41, bf16[512,512]{1,0:T(8,128)(2,1)S(1)} %all_gather.6), kind=kOutput, calls=%fused_computation.5 | convolution fusion | flops 268697600 | bytes 1572864 | tf_op jit(solution)/shard_map/dot_general | solution.py:39
  159.2 2.0 copy.14
  161.2 1.3 fusion.1
  162.5 2.0 copy.15
  164.5 2.3 %convolution_convert_fusion = bf16[512,512]{1,0:T(8,128)(2,1)} fusion(bf16[512,512]{1,0:T(8,128)(2,1)} %bitcast.42, bf16[512,512]{1,0:T(8,128)(2,1)S(1)} %all_gather.7), kind=kOutput, calls=%fused_computation.2 | convolution fusion | flops 268697600 | bytes 1572864 | tf_op jit(solution)/shard_map/dot_general | solution.py:45
  166.8 45.8 %all-to-all-done.2 = f32[32,16,512]{2,1,0:T(8,128)S(1)} async-done(((f32[32,16,512]{2,1,0:T(8,128)}), f32[32,16,512]{2,1,0:T(8,128)S(1)}, u32[]{:S(2)}, u32[]{:S(2)}) %all-to-all-start.2) | async-done | bytes 1048608 | tf_op jit(solution)/shard_map/all_to_all | solution.py:52
  212.6 0.7 reduce_sum.19
  (2 shorter events, 0.1 us)
Async XLA Ops:
  0.6 69.6 %copy-start = (bf16[512,512]{1,0:T(8,128)(2,1)S(1)}, bf16[512,512]{1,0:T(8,128)(2,1)}, u32[]{:S(2)}) copy-start(bf16[512,512]{1,0:T(8,128)(2,1)} %param.7) | copy-start | bytes 1572868
  0.6 70.1 %copy-start.3 = (bf16[512,512]{1,0:T(8,128)(2,1)S(1)}, bf16[512,512]{1,0:T(8,128)(2,1)}, u32[]{:S(2)}) copy-start(bf16[512,512]{1,0:T(8,128)(2,1)} %param.9) | copy-start | bytes 1572868
  144.4 1.4 copy-start.1
  145.3 1.9 copy-start.2
  147.3 65.3 %all-to-all-start.2 = ((f32[32,16,512]{2,1,0:T(8,128)}), f32[32,16,512]{2,1,0:T(8,128)S(1)}, u32[]{:S(2)}, u32[]{:S(2)}) async-start(f32[32,16,512]{2,1,0:T(8,128)} %bitcast.9), calls=%async_computation.2 | async-start | bytes 2097152 | tf_op jit(solution)/shard_map/all_to_all | solution.py:52
where the time goes:
time: 214 us; the launch traced here: 213 us
  blocking collectives  138 us (64%)
  waiting for transfers between devices  45.8 us (21%)
  matrix products  10.1 us (5%)
  starting transfers between devices  9.62 us (4%)
  local copies, waits for them, and re-layouts  5.2 us (2%)
  other arithmetic  3.47 us (2%)
    all_to_all x1, waiting for transfers between devices, body(): input_grad = lax.all_to_all(total, 'row', 0, 0, tiled=True).sum(axis=0)  45.8 us
    all_to_all x1, blocking collectives, body(): parts = lax.all_to_all(parts, 'col', 1, 1, tiled=True)  45.6 us
    all_gather x1, blocking collectives, body(): rows_all = lax.all_gather(tokens, 'row', axis=0, tiled=True)  39.4 us
    all_gather x1, blocking collectives, body(): grads_all = lax.all_gather(out_grad, 'row', axis=0, tiled=True)  28.7 us
    all_to_all x1, blocking collectives, body(): spread = lax.all_to_all(spread, 'col', 0, 0, tiled=True)  24.6 us
    all_to_all x1, starting transfers between devices, body(): input_grad = lax.all_to_all(total, 'row', 0, 0, tiled=True).sum(axis=0)  9.62 us
  transfers between devices with their start and end apart: 1, of which 1 were waited for; matrix products, arithmetic and copies ran while one was open for 5% of the time, Pallas kernels for 0%

commit v1 on v0

--- a/solution.py
+++ b/solution.py
@@ -2,6 +2,16 @@
 import jax.numpy as jnp
 from jax import lax
 from jax.sharding import PartitionSpec as P
+
+solve_arrays_now = lambda obj, net_axis: jnp.concatenate(
+    jax.lax.all_to_all(
+        jnp.stack([obj for _ in range(jax.lax.axis_size(net_axis))]),
+        net_axis,
+        split_axis=0,
+        concat_axis=0,
+    ),
+    0,
+)
 
 
 def pointwise(gate, up, hidden_grad):
@@ -17,7 +27,7 @@
     n_col = lax.psum(1, "col")
     n_row = lax.psum(1, "row")
     rows_all = lax.all_gather(tokens, "row", axis=0, tiled=True)
-    grads_all = lax.all_gather(out_grad, "row", axis=0, tiled=True)
+    grads_all = solve_arrays_now(out_grad, "row")
     n_tok, width = rows_all.shape
     contract_cols = (((1,), (1,)), ((), ()))
     contract_rows = (((0,), (0,)), ((), ()))

time: 214 us -> 220 us (1.028)
  starting transfers between devices: 9.62 us -> 29.4 us
  blocking collectives: 138 us -> 121 us
  waiting for transfers between devices: 45.8 us -> 48.5 us
    all_gather x1 -> x0, blocking collectives: 28.7 us -> none  [body(): grads_all = lax.all_gather(out_grad, 'row', axis=0, tiled=True)]
    all_to_all x0 -> x1, starting transfers between devices: none -> 16.8 us  [jax.lax.all_to_all(jnp.stack([obj for _ in range(jax.lax.axis_size(net_ax...]
    all_gather x1, blocking collectives: 39.4 us -> 51.2 us  [body(): rows_all = lax.all_gather(tokens, 'row', axis=0, tiled=True)]
    all_to_all x1, starting transfers between devices: 9.62 us -> 12.7 us  [body(): input_grad = lax.all_to_all(total, 'row', 0, 0, tiled=True).sum(axis=0)]
    all_to_all x1, waiting for transfers between devices: 45.8 us -> 48.5 us  [body(): input_grad = lax.all_to_all(total, 'row', 0, 0, tiled=True).sum(axis=0)]
  transfers between devices with their start and end apart: 1 -> 2, of which waited for: 1 -> 1; matrix products, arithmetic and copies ran while one was open for 5% -> 4% of each run, Pallas kernels for 0% -> 0%
where the time goes in v1:
time: 220 us; the launch traced here: 219 us
  blocking collectives  121 us (55%)
  waiting for transfers between devices  48.5 us (22%)
  starting transfers between devices  29.4 us (13%)
  matrix products  9.65 us (4%)
  local copies, waits for them, and re-layouts  6.3 us (3%)
  other arithmetic  3.31 us (2%)
    all_gather x1, blocking collectives, body(): rows_all = lax.all_gather(tokens, 'row', axis=0, tiled=True)  51.2 us
    all_to_all x1, waiting for transfers between devices, body(): input_grad = lax.all_to_all(total, 'row', 0, 0, tiled=True).sum(axis=0)  48.5 us
    all_to_all x1, blocking collectives, body(): parts = lax.all_to_all(parts, 'col', 1, 1, tiled=True)  45.6 us
    all_to_all x1, blocking collectives, body(): spread = lax.all_to_all(spread, 'col', 0, 0, tiled=True)  24.6 us
    all_to_all x1, starting transfers between devices, jax.lax.all_to_all(jnp.stack([obj for _ in range(jax.lax.axis_size(net_ax...  16.8 us
    all_to_all x1, starting transfers between devices, body(): input_grad = lax.all_to_all(total, 'row', 0, 0, tiled=True).sum(axis=0)  12.7 us
  transfers between devices with their start and end apart: 2, of which 1 were waited for; matrix products, arithmetic and copies ran while one was open for 4% of the time, Pallas kernels for 0%

profile of v1, /device:TPU:1, one launch (start us, length us, event | category | flops | bytes accessed | tf_op | source)
XLA Modules:
  0.0 219.4 jit_solution(3409906493292522678)
XLA Ops:
  0.6 0.0 copy-start
  0.6 1.6 stack.12
  2.3 16.8 %all-to-all-start = ((bf16[32,16,512]{2,1,0:T(8,128)(2,1)}), bf16[32,16,512]{2,1,0:T(8,128)(2,1)}, u32[]{:S(2)}, u32[]{:S(2)}) async-start(bf16[32,16,512]{2,1,0:T(8,128)(2,1)} %stack.12), calls=%async_computation | async-start | bytes 1048576 | tf_op jit(solution)/shard_map/all_to_all | solution.py:7
  19.1 51.2 %all_gather.3 = bf16[512,512]{1,0:T(8,128)(2,1)S(1)} all-gather(bf16[16,512]{1,0:T(8,128)(2,1)} %param.5), channel_id=1, replica_groups=mesh['row'=32,'col'=16] {'row'}, dimensions={0}, use_global_device_ids=true | all-gather | bytes 540672 | tf_op jit(solution)/shard_map/all_gather | solution.py:29
  70.3 1.5 fusion.6
  71.8 0.0 copy-done
  71.8 0.4 fusion.5
  72.2 0.0 all-to-all-done
  72.2 1.7 convolution_bitcast_fusion
  73.9 0.4 pad_maximum_fusion
  74.3 0.5 copy.11
  74.8 45.6 %all_to_all.20 = f32[3,16,32,512]{3,2,0,1:T(8,128)} all-to-all(f32[3,16,32,512]{3,2,0,1:T(8,128)S(1)} %copy.11), channel_id=1, replica_groups=mesh['row'=32,'col'=16] {'col'}, dimensions={1} | all-to-all | bytes 6291456 | tf_op jit(solution)/shard_map/all_to_all | solution.py:42
  120.5 2.2 %reduce_sum.18 = f32[3,32,512]{2,1,0:T(8,128)S(1)} reduce(f32[3,16,32,512]{3,2,0,1:T(8,128)} %all_to_all.20, f32[]{:T(128)} %constant.0.clone.1), dimensions={1}, to_apply=%region_0.0 | reduce | flops 737280 | bytes 3342340 | tf_op jit(solution)/shard_map/reduce_sum | solution.py:43
  122.7 0.2 broadcast_in_dim.2
  122.9 24.6 %all_to_all.21 = bf16[16,3,32,512]{3,2,1,0:T(8,128)(2,1)S(1)} all-to-all(bf16[16,3,32,512]{3,2,1,0:T(8,128)(2,1)S(1)} %broadcast_in_dim.2), channel_id=1, replica_groups=mesh['row'=32,'col'=16] {'col'}, dimensions={0} | all-to-all | bytes 3145728 | tf_op jit(solution)/shard_map/all_to_all | solution.py:46
  147.5 0.0 copy-start.1
  147.5 0.9 fusion.4
  148.4 0.5 fusion.7
  148.9 0.0 copy-done.1
  148.9 1.4 convolution_add_fusion
  150.3 12.7 %all-to-all-start.3 = ((f32[32,16,512]{2,1,0:T(8,128)}), f32[32,16,512]{2,1,0:T(8,128)S(1)}, u32[]{:S(2)}, u32[]{:S(2)}) async-start(f32[32,16,512]{2,1,0:T(8,128)} %bitcast.8), calls=%async_computation.3 | async-start | bytes 2097152 | tf_op jit(solution)/shard_map/all_to_all | solution.py:62
  163.0 1.3 fusion
  164.2 2.0 copy.12
  166.3 0.5 fusion.1
  166.7 1.0 copy.13
  167.8 2.5 %convolution_convert_fusion = bf16[512,512]{1,0:T(8,128)(2,1)} fusion(bf16[512,512]{1,0:T(8,128)(2,1)} %bitcast.40, bf16[512,512]{1,0:T(8,128)(2,1)} %bitcast.12), kind=kOutput, calls=%fused_computation.3 | convolution fusion | flops 268697600 | bytes 1572864 | tf_op jit(solution)/shard_map/dot_general | solution.py:55
  170.2 48.5 %all-to-all-done.3 = f32[32,16,512]{2,1,0:T(8,128)S(1)} async-done(((f32[32,16,512]{2,1,0:T(8,128)}), f32[32,16,512]{2,1,0:T(8,128)S(1)}, u32[]{:S(2)}, u32[]{:S(2)}) %all-to-all-start.3) | async-done | bytes 1048608 | tf_op jit(solution)/shard_map/all_to_all | solution.py:62
  218.7 0.7 reduce_sum.19
  (2 shorter events, 0.1 us)
Async XLA Ops:
  0.6 71.1 %copy-start = (bf16[512,512]{1,0:T(8,128)(2,1)S(1)}, bf16[512,512]{1,0:T(8,128)(2,1)}, u32[]{:S(2)}) copy-start(bf16[512,512]{1,0:T(8,128)(2,1)} %param.7) | copy-start | bytes 1572868
  2.3 69.9 %all-to-all-start = ((bf16[32,16,512]{2,1,0:T(8,128)(2,1)}), bf16[32,16,512]{2,1,0:T(8,128)(2,1)}, u32[]{:S(2)}, u32[]{:S(2)}) async-start(bf16[32,16,512]{2,1,0:T(8,128)(2,1)} %stack.12), calls=%async_computation | async-start | bytes 1048576 | tf_op jit(solution)/shard_map/all_to_all | solution.py:7
  147.5 1.4 copy-start.1
  150.3 68.4 %all-to-all-start.3 = ((f32[32,16,512]{2,1,0:T(8,128)}), f32[32,16,512]{2,1,0:T(8,128)S(1)}, u32[]{:S(2)}, u32[]{:S(2)}) async-start(f32[32,16,512]{2,1,0:T(8,128)} %bitcast.8), calls=%async_computation.3 | async-start | bytes 2097152 | tf_op jit(solution)/shard_map/all_to_all | solution.py:62
